TPU v7x, 32 devices: a whole 2x2x4 slice. The times are simulated.
32 devices in a mesh: crop: 8 (over z, y), head: 4 (over x, core).
Axes of the slice: x: 2, y: 2, z: 4, core: 2. Of those that a mesh axis runs over, the one named last changes fastest.
Arguments:
- global_rows: bfloat16 [4096, 4096], P('crop', 'head'), may hold values from -6 to 6
- crop_tokens: bfloat16 [8192, 4096], P('crop', 'head'), may hold values from -6 to 6
- query_weight: bfloat16 [4096, 4096], P('crop', 'head'), may hold values from -0.125 to 0.125
- key_weight: bfloat16 [4096, 4096], P('crop', 'head'), may hold values from -0.125 to 0.125
- value_weight: bfloat16 [4096, 4096], P('crop', 'head'), may hold values from -0.09375 to 0.09375
- fetch_slots: int32 [8, 8, 2], P('crop'), may hold values from 0 to 63
- region_slots: int32 [128, 8], P('crop'), may hold values from 0 to 15, as said below
- region_len: int32 [128], P('crop'), may hold values from 4 to 8
Outputs:
- attended: bfloat16 [4096, 4096], P('crop', 'head')
Inputs may be any that keep to these rules, and one draw needn't show every extreme that they name: `fetch_slots`: entry [s, o, c] numbers one of the 64 crop blocks of index s of crop. `region_slots`: the blocks listed for one page-row are distinct; the lists of the 16 page-rows of one index of crop together name all 16 delivered blocks. page-row r uses its first region_len[r] listed blocks.
All inputs are finite; a program needn't handle non-finite values.
Results may differ from a plain program's by a relative error of at most 0.008.
Values may be sent and summed in bfloat16 or wider, within the bound.
No kernel may reach another device: no remote copies, remote signals or barrier semaphores. Data moves between devices by JAX's collectives and lax.ppermute only.
A program may use at most 128 MiB of HBM per device.

v0:
```python
import jax
import jax.numpy as jnp
from jax import lax
from jax.sharding import PartitionSpec as P

HD = 128
CT = 16
CAP = 2
NB = 8
GR = 32


def add_rows(left, piece):
    return jnp.dot(left, piece, preferred_element_type=jnp.float32)


def body(
    global_rows,
    crop_tokens,
    query_weight,
    key_weight,
    value_weight,
    fetch_slots,
    region_slots,
    region_len,
):
    width = key_weight.shape[1]
    heads_here = width // HD
    ncrop = lax.axis_size("crop")
    rows_here = region_slots.shape[0]
    queries_in = lax.all_gather(global_rows, "head", axis=1, tiled=True)
    query = add_rows(queries_in, lax.all_gather(query_weight, "crop", axis=0, tiled=True)).astype(
        jnp.bfloat16
    )
    picks = fetch_slots[0]
    tokens_all = lax.all_gather(crop_tokens, "head", axis=1, tiled=True)

    def add_one(piece):
        return add_rows(tokens_all, piece)

    keys_full = add_one(lax.all_gather(key_weight, "crop", axis=0, tiled=True))
    vals_full = add_one(lax.all_gather(value_weight, "crop", axis=0, tiled=True))
    packed = jnp.concatenate(
        [keys_full.astype(jnp.bfloat16), vals_full.astype(jnp.bfloat16)], axis=1
    )
    packed = packed.reshape(-1, CT, 2 * width)
    outgoing = packed[picks]
    incoming = lax.all_to_all(outgoing, "crop", split_axis=0, concat_axis=0, tiled=True)
    slotted = incoming.reshape(ncrop * CAP, CT, 2 * width)
    listed = slotted[region_slots].reshape(rows_here, NB * CT, 2 * width)
    keys_row = listed[:, :, :width].reshape(rows_here, NB * CT, heads_here, HD)
    vals_row = listed[:, :, width:].reshape(rows_here, NB * CT, heads_here, HD)
    query_row = query.reshape(rows_here, GR, heads_here, HD)
    scale = 1.0 / HD**0.5
    scores = (
        jnp.einsum("rghe,rkhe->rhgk", query_row, keys_row, preferred_element_type=jnp.float32)
        * scale
    )
    used = (jnp.arange(NB * CT, dtype=jnp.int32) // CT)[None, :] < region_len[:, None]
    scores = jnp.where(used[:, None, None, :], scores, jnp.float32(-1e30))
    top = jnp.max(scores, axis=-1, keepdims=True)
    expo = jnp.exp(scores - top)
    weights = (expo / jnp.sum(expo, axis=-1, keepdims=True)).astype(jnp.bfloat16)
    result = jnp.einsum("rhgk,rkhe->rghe", weights, vals_row, preferred_element_type=jnp.float32)
    return result.astype(jnp.bfloat16).reshape(rows_here * GR, width)


def solution(mesh):
    placed = (
        P("crop", "head"),
        P("crop", "head"),
        P("crop", "head"),
        P("crop", "head"),
        P("crop", "head"),
        P("crop", None, None),
        P("crop", None),
        P("crop"),
    )
    return jax.shard_map(
        body, mesh=mesh, in_specs=placed, out_specs=P("crop", "head"), check_vma=False
    )
```

profile of v0, /device:TPU:0, one launch (start us, length us, event | category | flops | bytes accessed | tf_op | source)
XLA Modules:
  0.0 549.0 jit_solution(13589215673044014440)
XLA Ops:
  6.5 0.0 copy-start.2
  6.5 0.0 copy-start.1
  6.5 0.0 all-gather.6.cloned.1.call-start
  6.5 0.7 all-gather.6.cloned.1.call-update
  7.3 0.0 all-gather.8.cloned.1.call-start
  7.3 0.7 all-gather.8.cloned.1.call-update
  8.0 0.0 all-gather.10.cloned.1.call-start
  8.1 0.7 all-gather.10.cloned.1.call-update
  8.7 0.0 all-gather.12.cloned.1.call-start
  8.8 0.5 all-gather.12.cloned.1.call-update
  9.3 0.0 all-gather.14.cloned.1.call-start
  9.4 0.5 all-gather.14.cloned.1.call-update
  9.9 0.0 copy-done.2
  9.9 0.1 copy.13
  10.0 0.1 reshape.96
  10.1 0.0 copy-done.1
  10.1 0.1 copy.14
  10.2 0.1 reshape.104
  10.3 59.6 %all-gather.6.cloned.1.call-done = bf16[1024,4096]{1,0:T(8,128)(2,1)} async-done(((bf16[1024,1024]{1,0:T(8,128)(2,1)}), bf16[1024,4096]{1,0:T(8,128)(2,1)}) %all-gather.6.cloned.1.call-update) | async-done | bytes 8388624 | tf_op jit(solution)/shard_map/all_gather | solution.py:36
  69.9 127.1 %all-gather.8.cloned.1.call-done = bf16[4096,1024]{1,0:T(8,128)(2,1)} async-done(((bf16[512,1024]{1,0:T(8,128)(2,1)}), bf16[4096,1024]{1,0:T(8,128)(2,1)}) %all-gather.8.cloned.1.call-update) | async-done | bytes 8388624 | tf_op jit(solution)/shard_map/all_gather | solution.py:41
  197.0 13.7 %convolution_convert_fusion.1 = bf16[1024,1024]{0,1:T(8,128)(2,1)S(1)} fusion(bf16[1024,4096]{1,0:T(8,128)(2,1)} %all-gather.6.cloned.1.call-done, bf16[4096,1024]{1,0:T(8,128)(2,1)} %all-gather.8.cloned.1.call-done), kind=kOutput, calls=%fused_computation.8 | convolution fusion | flops 8590983168 | bytes 18874368 | tf_op jit(solution)/shard_map/dot_general | solution.py:14
  210.8 111.5 %all-gather.10.cloned.1.call-done = bf16[4096,1024]{1,0:T(8,128)(2,1)} async-done(((bf16[512,1024]{1,0:T(8,128)(2,1)}), bf16[4096,1024]{1,0:T(8,128)(2,1)}) %all-gather.10.cloned.1.call-update) | async-done | bytes 8388624 | tf_op jit(solution)/shard_map/all_gather | solution.py:42
  322.3 13.7 %convolution_convert_fusion = bf16[1024,1024]{0,1:T(8,128)(2,1)S(1)} fusion(bf16[1024,4096]{1,0:T(8,128)(2,1)} %all-gather.6.cloned.1.call-done, bf16[4096,1024]{1,0:T(8,128)(2,1)} %all-gather.10.cloned.1.call-done), kind=kOutput, calls=%fused_computation.7 | convolution fusion | flops 8590983168 | bytes 18874368 | tf_op jit(solution)/shard_map/dot_general | solution.py:14
  336.1 2.4 pad_maximum_fusion
  338.5 6.6 %copy.12 = bf16[1024,2048]{1,0:T(8,128)(2,1)} copy(bf16[1024,2048]{0,1:T(8,128)(2,1)} %pad_maximum_fusion) | data formatting | bytes 8388608 | tf_op jit(solution)/shard_map/concatenate | solution.py:43
  345.1 0.0 copy-start.3
  345.1 3.8 gather_fusion
  348.9 3.7 all-to-all-start
  352.6 0.0 copy-done.3
  352.6 0.1 broadcast_compare_fusion
  352.7 3.7 all-gather.12.cloned.1.call-done
  356.4 133.9 %all-gather.14.cloned.1.call-done = bf16[4096,1024]{1,0:T(8,128)(2,1)} async-done(((bf16[512,1024]{1,0:T(8,128)(2,1)}), bf16[4096,1024]{1,0:T(8,128)(2,1)}) %all-gather.14.cloned.1.call-update) | async-done | bytes 8388624 | tf_op jit(solution)/shard_map/all_gather | solution.py:32
  490.3 9.1 %fusion.3 = bf16[64,8,8,128]{3,1,2,0:T(8,128)(2,1)S(1)} fusion(bf16[512,4096]{1,0:T(8,128)(2,1)} %all-gather.12.cloned.1.call-done, bf16[4096,1024]{1,0:T(8,128)(2,1)} %all-gather.14.cloned.1.call-done), kind=kOutput, calls=%fused_computation.13 | convolution fusion | flops 4295491584 | bytes 13631488 | tf_op jit(solution)/shard_map/dot_general | solution.py:14
  499.4 0.3 copy.23
  499.7 0.0 all-to-all-done
  499.7 6.2 %gather_fusion.1 = bf16[128,16,2048]{2,1,0:T(8,128)(2,1)} fusion(bf16[16,16,2048]{2,1,0:T(8,128)(2,1)S(1)} %bitcast.29, s32[1024]{0:T(1024)S(1)} %pad_clamp_fusion), kind=kCustom, calls=%fused_computation.1 | custom fusion | bytes 16777728 | tf_op jit(solution)/shard_map/gather | solution.py:50
  506.0 6.0 %fusion.17 = (bf16[16,128,1024]{2,1,0:T(8,128)(2,1)}, bf16[16,128,1024]{2,1,0:T(8,128)(2,1)}) fusion(bf16[16,128,2048]{2,1,0:T(8,128)(2,1)} %bitcast.30), kind=kLoop, calls=%fused_computation.35 | loop fusion | bytes 16777216 | tf_op jit(solution)/shard_map/slice | solution.py:51
  512.0 6.4 %copy.16 = bf16[16,128,1024]{1,2,0:T(8,128)(2,1)} copy(bf16[16,128,1024]{2,1,0:T(8,128)(2,1)} %get-tuple-element.5) | data formatting | bytes 8388608 | tf_op jit(solution)/shard_map/slice | solution.py:51
  518.4 6.4 %copy.15 = bf16[16,128,1024]{1,2,0:T(8,128)(2,1)} copy(bf16[16,128,1024]{2,1,0:T(8,128)(2,1)} %get-tuple-element.6) | data formatting | bytes 8388608 | tf_op jit(solution)/shard_map/slice | solution.py:52
  524.8 3.4 fusion.4
  528.2 0.0 copy-start
  528.2 1.3 copy-done
  529.5 1.2 fusion.18
  530.7 10.1 %fusion.2 = bf16[16,32,8,128]{3,1,2,0:T(8,128)(2,1)S(1)} fusion(bf16[16,128,8,128]{1,3,2,0:T(8,128)(2,1)} %bitcast.34, f32[16,8,32]{2,1,0:T(8,128)S(1)} %fusion.18, f32[16,8,32,128]{3,2,1,0:T(8,128)} %copy-done, pred[16,128]{1,0:T(8,128)(4,1)S(1)} %broadcast_compare_fusion), kind=kOutput, calls=%fused_computation.12 | convolution fusion | flops 137367680 | bytes 7358464 | tf_op jit(solution)/shard_map/rhgk,rkhe->rghe/dot_general | solution.py:64
  540.8 0.5 copy.20
  541.2 1.2 copy.28
  (5 shorter events, 0.0 us)
Async XLA Ops:
  6.5 3.4 copy-start.2
  6.5 3.6 copy-start.1
  6.5 63.4 %all-gather.6.cloned.1.call-start = ((), (), s32[]{:S(2)}) async-start(), calls=%async_computation.1 | async-start | bytes 10485760 | tf_op jit(solution)/shard_map/all_gather | solution.py:36
  7.3 189.8 %all-gather.8.cloned.1.call-start = ((), (), s32[]{:S(2)}) async-start(), calls=%async_computation.2 | async-start | bytes 9437184 | tf_op jit(solution)/shard_map/all_gather | solution.py:41
  8.0 314.3 %all-gather.10.cloned.1.call-start = ((), (), s32[]{:S(2)}) async-start(), calls=%async_computation.3 | async-start | bytes 9437184 | tf_op jit(solution)/shard_map/all_gather | solution.py:42
  8.7 347.7 %all-gather.12.cloned.1.call-start = ((), (), s32[]{:S(2)}) async-start(), calls=%async_computation.4 | async-start | bytes 5242880 | tf_op jit(solution)/shard_map/all_gather | solution.py:31
  9.3 481.0 %all-gather.14.cloned.1.call-start = ((), (), s32[]{:S(2)}) async-start(), calls=%async_computation.5 | async-start | bytes 9437184 | tf_op jit(solution)/shard_map/all_gather | solution.py:32
  345.1 7.5 %copy-start.3 = (s32[16]{0:T(128)S(1)}, s32[16]{0:T(128)}, u32[]{:S(2)}) copy-start(s32[16]{0:T(128)} %param.15) | copy-start | bytes 196
  348.9 150.9 %all-to-all-start = ((bf16[8,2,16,2048]{3,2,1,0:T(8,128)(2,1)}), bf16[8,2,16,2048]{3,2,1,0:T(8,128)(2,1)S(1)}, u32[]{:S(2)}, u32[]{:S(2)}) async-start(bf16[8,2,16,2048]{3,2,1,0:T(8,128)(2,1)} %bitcast.2), calls=%async_computation | async-start | bytes 2097152 | tf_op jit(solution)/shard_map/all_to_all | solution.py:48
  528.2 1.3 copy-start
Sparse Core Ops, SparseCore 0:
  8.9 60.9 all-gather.5
  72.1 124.9 all-gather.7
  199.2 123.1 all-gather.9
  323.7 32.6 all-gather.11
  358.4 131.8 all-gather.13
where the time goes:
time: 550 us; the launch traced here: 549 us
  waiting for transfers between devices  439 us (80%)
  matrix products  50.1 us (9%)
  local copies, waits for them, and re-layouts  39.1 us (7%)
  between operations  13.3 us (2%)
    all_gather x1, waiting for transfers between devices, body(): lax.all_gather(query_weight, 'crop', axis=0, tiled=True)  134 us
    all_gather x1, waiting for transfers between devices, body(): keys_full = add_one(lax.all_gather(key_weight, 'crop', axis=0, tiled=True))  127 us
    all_gather x1, waiting for transfers between devices, body(): lax.all_gather(value_weight, 'crop', axis=0, tiled=True)  112 us
    all_gather x1, waiting for transfers between devices, body(): tokens_all = lax.all_gather(crop_tokens, 'head', axis=1, tiled=True)  59.6 us
    dot_general x3, matrix products, add_rows(): return jnp.dot(left, piece, preferred_element_type=jnp.float32)  36.6 us
    slice x2, local copies, waits for them, and re-layouts, body(): keys_row = listed[:, :, :width].reshape(rows_here, NB * CT, heads_here, HD)  12.4 us
  transfers between devices with their start and end apart: 6, of which 5 were waited for; matrix products, arithmetic and copies ran while one was open for 9% of the time, Pallas kernels for 0%

commit v1 on v0

--- a/solution.py
+++ b/solution.py
@@ -1,3 +1,4 @@
+import functools
 import jax
 import jax.numpy as jnp
 from jax import lax
@@ -8,6 +9,32 @@
 CAP = 2
 NB = 8
 GR = 32
+
+
+def table_draft(mat, lane_axis):
+    newest, v_next, big = (
+        jax.lax.axis_size(lane_axis),
+        jax.lax.axis_index(lane_axis),
+        mat.shape[0],
+    )
+    lanes = tuple(((i0, (i0 + 1) % newest) for i0 in range(newest)))
+    cards = tuple(((i0, (i0 - 1) % newest) for i0 in range(newest)))
+    outer = jnp.zeros((*mat.shape[:0], newest * big, *mat.shape[1:]), mat.dtype)
+    outer = lax.dynamic_update_slice_in_dim(outer, mat, v_next * big, axis=0)
+    left_arr = res = mat
+    small = newest // 2
+    for m in range(1, small + 1):
+        left_arr = jax.lax.ppermute(left_arr, lane_axis, lanes)
+        outer = lax.dynamic_update_slice_in_dim(
+            outer, left_arr, (v_next - m) % newest * big, axis=0
+        )
+        if m < newest - small:
+            res = jax.lax.ppermute(res, lane_axis, cards)
+            outer = lax.dynamic_update_slice_in_dim(outer, res, (v_next + m) % newest * big, axis=0)
+    return outer
+
+
+_begin_surface = functools.partial(table_draft, lane_axis="crop")
 
 
 def add_rows(left, piece):
@@ -29,9 +56,7 @@
     ncrop = lax.axis_size("crop")
     rows_here = region_slots.shape[0]
     queries_in = lax.all_gather(global_rows, "head", axis=1, tiled=True)
-    query = add_rows(queries_in, lax.all_gather(query_weight, "crop", axis=0, tiled=True)).astype(
-        jnp.bfloat16
-    )
+    query = add_rows(queries_in, _begin_surface(query_weight)).astype(jnp.bfloat16)
     picks = fetch_slots[0]
     tokens_all = lax.all_gather(crop_tokens, "head", axis=1, tiled=True)
 

time: 550 us -> 494 us (0.90)
  waiting for transfers between devices: 439 us -> 343 us
  starting transfers between devices: 3.89 us -> 24.5 us
  local copies, waits for them, and re-layouts: 39.1 us -> 58.7 us
    ppermute x0 -> x7, waiting for transfers between devices: none -> 137 us  [the longest x4 137 us: table_draft(): left_arr = jax.lax.ppermute(left_arr, lane_axis, lanes)]
    all_gather x1 -> x0, waiting for transfers between devices: 134 us -> none  [body(): lax.all_gather(query_weight, 'crop', axis=0, tiled=True)]
    all_gather x1, waiting for transfers between devices: 59.6 us -> 0.01 us  [body(): tokens_all = lax.all_gather(crop_tokens, 'head', axis=1, tiled=True)]
    all_gather x1, waiting for transfers between devices: 112 us -> 84.1 us  [body(): lax.all_gather(value_weight, 'crop', axis=0, tiled=True)]
    ppermute x0 -> x7, starting transfers between devices: none -> 20.6 us  [the longest x4 11.4 us: table_draft(): left_arr = jax.lax.ppermute(left_arr, lane_axis, lanes)]
    all_gather x1, waiting for transfers between devices: 127 us -> 112 us  [body(): keys_full = add_one(lax.all_gather(key_weight, 'crop', axis=0, tiled=True))]
    dynamic_update_slice x0 -> x8, local copies, waits for them, and re-layouts: none -> 14.7 us  [the longest x4 7.93 us: table_draft(): lax.dynamic_update_slice_in_dim(outer, left_arr, (v_next - m) % newest *...]
    all_to_all x1, waiting for transfers between devices: 0.01 us -> 7.5 us  [body(): lax.all_to_all(outgoing, 'crop', split_axis=0, concat_axis=0, tiled=True)]
  transfers between devices with their start and end apart: 6 -> 12, of which waited for: 5 -> 6; matrix products, arithmetic and copies ran while one was open for 9% -> 14% of each run, Pallas kernels for 0% -> 0%
where the time goes in v1:
time: 494 us; the launch traced here: 493 us
  waiting for transfers between devices  343 us (69%)
  local copies, waits for them, and re-layouts  58.7 us (12%)
  matrix products  50.1 us (10%)
  starting transfers between devices  24.5 us (5%)
  between operations  13.3 us (3%)
    ppermute x4, waiting for transfers between devices, table_draft(): left_arr = jax.lax.ppermute(left_arr, lane_axis, lanes)  137 us
    all_gather x1, waiting for transfers between devices, body(): keys_full = add_one(lax.all_gather(key_weight, 'crop', axis=0, tiled=True))  112 us
    all_gather x1, waiting for transfers between devices, body(): lax.all_gather(value_weight, 'crop', axis=0, tiled=True)  84.1 us
    dot_general x3, matrix products, add_rows(): return jnp.dot(left, piece, preferred_element_type=jnp.float32)  36.6 us
    slice x2, local copies, waits for them, and re-layouts, body(): keys_row = listed[:, :, :width].reshape(rows_here, NB * CT, heads_here, HD)  12.5 us
    ppermute x4, starting transfers between devices, table_draft(): left_arr = jax.lax.ppermute(left_arr, lane_axis, lanes)  11.4 us
    dot_general x1, matrix products, body(): jnp.einsum('rhgk,rkhe->rghe', weights, vals_row, preferred_element_type=j...  10.1 us
  transfers between devices with their start and end apart: 12, of which 6 were waited for; matrix products, arithmetic and copies ran while one was open for 14% of the time, Pallas kernels for 0%

profile of v1, /device:TPU:0, one launch (start us, length us, event | category | flops | bytes accessed | tf_op | source)
XLA Modules:
  0.0 493.1 jit_solution(6317913797107463924)
XLA Ops:
  6.5 0.0 copy-start.1
  6.5 0.0 all-gather.5.cloned.1.call-start
  6.5 0.7 all-gather.5.cloned.1.call-update
  7.3 0.0 all-gather.9.cloned.1.call-start
  7.3 0.7 all-gather.9.cloned.1.call-update
  8.0 0.0 all-gather.7.cloned.1.call-start
  8.1 0.7 all-gather.7.cloned.1.call-update
  8.7 0.0 all-gather.11.cloned.1.call-start
  8.8 0.0 copy-done.1
  8.8 3.0 collective-permute-start
  11.8 3.1 collective-permute-start.1
  14.9 41.8 %collective-permute-done = bf16[512,1024]{1,0:T(8,128)(2,1)} collective-permute-done((bf16[512,1024]{1,0:T(8,128)(2,1)S(1)}, bf16[512,1024]{1,0:T(8,128)(2,1)}, u32[]{:S(2)}, u32[]{:S(2)}) %collective-permute-start) | collective-permute-done | bytes 1048608 | tf_op jit(solution)/shard_map/ppermute | solution.py:27
  56.7 2.6 collective-permute-start.2
  59.3 0.0 all-gather.11.cloned.1.call-update
  59.3 0.0 copy-done.2
  59.3 0.0 collective-permute-done.1
  59.4 3.1 collective-permute-start.3
  62.4 0.0 copy-done.3
  62.5 52.4 %collective-permute-done.2 = bf16[512,1024]{1,0:T(8,128)(2,1)S(1)} collective-permute-done((bf16[512,1024]{1,0:T(8,128)(2,1)}, bf16[512,1024]{1,0:T(8,128)(2,1)S(1)}, u32[]{:S(2)}, u32[]{:S(2)}) %collective-permute-start.2) | collective-permute-done | bytes 1048608 | tf_op jit(solution)/shard_map/ppermute | solution.py:27
  114.9 2.4 collective-permute-start.4
  117.2 0.1 copy.13
  117.3 0.1 reshape.96
  117.4 0.1 copy.14
  117.5 0.1 reshape.104
  117.6 0.0 copy-start.4
  117.7 4.3 broadcast_in_dim.26
  122.0 1.1 constant_dynamic-update-slice_fusion.7
  123.1 0.0 copy-done.4
  123.1 0.1 broadcast_compare_fusion
  123.2 2.3 constant_dynamic-update-slice_fusion.6
  125.5 2.3 constant_dynamic-update-slice_fusion.5
  127.7 0.0 collective-permute-done.3
  127.7 3.0 collective-permute-start.5
  130.8 1.1 constant_dynamic-update-slice_fusion.4
  131.8 43.3 %collective-permute-done.4 = bf16[512,1024]{1,0:T(8,128)(2,1)} collective-permute-done((bf16[512,1024]{1,0:T(8,128)(2,1)S(1)}, bf16[512,1024]{1,0:T(8,128)(2,1)}, u32[]{:S(2)}, u32[]{:S(2)}) %collective-permute-start.4) | collective-permute-done | bytes 1048608 | tf_op jit(solution)/shard_map/ppermute | solution.py:27
  175.1 3.4 collective-permute-start.6
  178.5 84.1 %all-gather.9.cloned.1.call-done = bf16[4096,1024]{1,0:T(8,128)(2,1)} async-done(((bf16[512,1024]{1,0:T(8,128)(2,1)}), bf16[4096,1024]{1,0:T(8,128)(2,1)}) %all-gather.9.cloned.1.call-update) | async-done | bytes 8388624 | tf_op jit(solution)/shard_map/all_gather | solution.py:67
  262.6 13.8 %convolution_convert_fusion = bf16[1024,1024]{0,1:T(8,128)(2,1)S(1)} fusion(bf16[1024,4096]{1,0:T(8,128)(2,1)} %all-gather.5.cloned.1.call-done, bf16[4096,1024]{1,0:T(8,128)(2,1)} %all-gather.9.cloned.1.call-done), kind=kOutput, calls=%fused_computation.7 | convolution fusion | flops 8590983168 | bytes 18874368 | tf_op jit(solution)/shard_map/dot_general | solution.py:41
  276.3 111.7 %all-gather.7.cloned.1.call-done = bf16[4096,1024]{1,0:T(8,128)(2,1)} async-done(((bf16[512,1024]{1,0:T(8,128)(2,1)}), bf16[4096,1024]{1,0:T(8,128)(2,1)}) %all-gather.7.cloned.1.call-update) | async-done | bytes 8388624 | tf_op jit(solution)/shard_map/all_gather | solution.py:66
  388.0 13.7 %convolution_convert_fusion.1 = bf16[1024,1024]{0,1:T(8,128)(2,1)S(1)} fusion(bf16[1024,4096]{1,0:T(8,128)(2,1)} %all-gather.5.cloned.1.call-done, bf16[4096,1024]{1,0:T(8,128)(2,1)} %all-gather.7.cloned.1.call-done), kind=kOutput, calls=%fused_computation.8 | convolution fusion | flops 8590983168 | bytes 18874368 | tf_op jit(solution)/shard_map/dot_general | solution.py:41
  401.8 2.5 pad_maximum_fusion
  404.3 6.6 %copy.12 = bf16[1024,2048]{1,0:T(8,128)(2,1)} copy(bf16[1024,2048]{0,1:T(8,128)(2,1)} %pad_maximum_fusion) | data formatting | bytes 8388608 | tf_op jit(solution)/shard_map/concatenate | solution.py:68
  410.9 3.8 gather_fusion
  414.6 3.7 all-to-all-start
  418.4 1.1 constant_dynamic-update-slice_fusion.3
  419.4 2.3 constant_dynamic-update-slice_fusion.2
  421.7 0.0 collective-permute-done.5
  421.7 2.3 constant_dynamic-update-slice_fusion.1
  424.0 0.0 collective-permute-done.6
  424.0 2.3 constant_dynamic-update-slice_fusion
  426.3 9.1 %fusion.3 = bf16[512,1024]{0,1:T(8,128)(2,1)S(1)} fusion(bf16[4096,1024]{1,0:T(8,128)(2,1)} %constant_dynamic-update-slice_fusion, bf16[512,4096]{1,0:T(8,128)(2,1)} %all-gather.11.cloned.1.call-done), kind=kOutput, calls=%fused_computation.13 | convolution fusion | flops 4295491584 | bytes 13631488 | tf_op jit(solution)/shard_map/dot_general | solution.py:41
  435.4 0.5 copy.16
  436.0 0.3 copy.24
  436.3 7.5 %all-to-all-done = bf16[8,2,16,2048]{3,2,1,0:T(8,128)(2,1)S(1)} async-done(((bf16[8,2,16,2048]{3,2,1,0:T(8,128)(2,1)}), bf16[8,2,16,2048]{3,2,1,0:T(8,128)(2,1)S(1)}, u32[]{:S(2)}, u32[]{:S(2)}) %all-to-all-start) | async-done | bytes 1048608 | tf_op jit(solution)/shard_map/all_to_all | solution.py:73
  443.8 6.2 %gather_fusion.1 = bf16[128,16,2048]{2,1,0:T(8,128)(2,1)} fusion(bf16[16,16,2048]{2,1,0:T(8,128)(2,1)S(1)} %bitcast.30, s32[1024]{0:T(1024)S(1)} %pad_clamp_fusion), kind=kCustom, calls=%fused_computation.1 | custom fusion | bytes 16777728 | tf_op jit(solution)/shard_map/gather | solution.py:75
  450.0 6.0 %fusion.17 = (bf16[16,128,1024]{2,1,0:T(8,128)(2,1)}, bf16[16,128,1024]{2,1,0:T(8,128)(2,1)}) fusion(bf16[16,128,2048]{2,1,0:T(8,128)(2,1)} %bitcast.31), kind=kLoop, calls=%fused_computation.43 | loop fusion | bytes 16777216 | tf_op jit(solution)/shard_map/slice | solution.py:76
  456.0 6.4 %copy.17 = bf16[16,128,1024]{1,2,0:T(8,128)(2,1)} copy(bf16[16,128,1024]{2,1,0:T(8,128)(2,1)} %get-tuple-element.5) | data formatting | bytes 8388608 | tf_op jit(solution)/shard_map/slice | solution.py:76
  462.5 6.4 %copy.15 = bf16[16,128,1024]{1,2,0:T(8,128)(2,1)} copy(bf16[16,128,1024]{2,1,0:T(8,128)(2,1)} %get-tuple-element.6) | data formatting | bytes 8388608 | tf_op jit(solution)/shard_map/slice | solution.py:77
  468.9 3.4 fusion.4
  472.3 1.4 copy-done
  473.6 1.2 fusion.18
  474.8 10.1 %fusion.2 = bf16[16,32,8,128]{3,1,2,0:T(8,128)(2,1)S(1)} fusion(bf16[16,128,8,128]{1,3,2,0:T(8,128)(2,1)} %bitcast.35, f32[16,8,32]{2,1,0:T(8,128)S(1)} %fusion.18, f32[16,8,32,128]{3,2,1,0:T(8,128)} %copy-done, pred[16,128]{1,0:T(8,128)(4,1)S(1)} %broadcast_compare_fusion), kind=kOutput, calls=%fused_computation.12 | convolution fusion | flops 137367680 | bytes 7358464 | tf_op jit(solution)/shard_map/rhgk,rkhe->rghe/dot_general | solution.py:89
  484.9 0.5 copy.21
  485.3 1.2 copy.29
  (10 shorter events, 0.0 us)
Async XLA Ops:
  6.5 2.3 copy-start.1
  6.5 52.8 %copy-start.2 = (s32[16,8]{0,1:T(8,128)S(1)}, s32[16,8]{0,1:T(8,128)}, u32[]{:S(2)}) copy-start(s32[16,8]{0,1:T(8,128)} %param.14) | copy-start | bytes 1540
  6.5 55.9 %copy-start.3 = (s32[1,8,2]{1,2,0:T(2,128)S(1)}, s32[1,8,2]{1,2,0:T(2,128)}, u32[]{:S(2)}) copy-start(s32[1,8,2]{1,2,0:T(2,128)} %param.13) | copy-start | bytes 196
  6.5 172.0 %all-gather.5.cloned.1.call-start = ((), (), s32[]{:S(2)}) async-start(), calls=%async_computation.1 | async-start | bytes 10485760 | tf_op jit(solution)/shard_map/all_gather | solution.py:61
  7.3 255.3 %all-gather.9.cloned.1.call-start = ((), (), s32[]{:S(2)}) async-start(), calls=%async_computation.3 | async-start | bytes 9437184 | tf_op jit(solution)/shard_map/all_gather | solution.py:67
  8.0 380.0 %all-gather.7.cloned.1.call-start = ((), (), s32[]{:S(2)}) async-start(), calls=%async_computation.2 | async-start | bytes 9437184 | tf_op jit(solution)/shard_map/all_gather | solution.py:66
  8.7 417.6 %all-gather.11.cloned.1.call-start = ((), (), s32[]{:S(2)}) async-start(), calls=%async_computation.4 | async-start | bytes 5242880 | tf_op jit(solution)/shard_map/all_gather | solution.py:58
  8.8 47.9 %collective-permute-start = (bf16[512,1024]{1,0:T(8,128)(2,1)S(1)}, bf16[512,1024]{1,0:T(8,128)(2,1)}, u32[]{:S(2)}, u32[]{:S(2)}) collective-permute-start(bf16[512,1024]{1,0:T(8,128)(2,1)S(1)} %copy-done.1), channel_id=1, source_target_pairs={{0,4},{4,8},{8,12},{12,16},{16,20},{20,24},{24,28},{28,0},{1,5},{5... | collective-permute-start | bytes 3145736 | tf_op jit(solution)/shard_map/ppermute | solution.py:27
  11.8 47.5 %collective-permute-start.1 = (bf16[512,1024]{1,0:T(8,128)(2,1)S(1)}, bf16[512,1024]{1,0:T(8,128)(2,1)}, u32[]{:S(2)}, u32[]{:S(2)}) collective-permute-start(bf16[512,1024]{1,0:T(8,128)(2,1)S(1)} %copy-done.1), channel_id=1, source_target_pairs={{0,28},{4,0},{8,4},{12,8},{16,12},{20,16},{24,20},{28,24},{1,29},{... | collective-permute-start | bytes 3145736 | tf_op jit(solution)/shard_map/ppermute | solution.py:32
  56.7 58.2 %collective-permute-start.2 = (bf16[512,1024]{1,0:T(8,128)(2,1)}, bf16[512,1024]{1,0:T(8,128)(2,1)S(1)}, u32[]{:S(2)}, u32[]{:S(2)}) collective-permute-start(bf16[512,1024]{1,0:T(8,128)(2,1)} %collective-permute-done), channel_id=1, source_target_pairs={{0,4},{4,8},{8,12},{12,16},{16,20},{20,24},{24,28},{28,0},{1,5},{5... | collective-permute-start | bytes 3145736 | tf_op jit(solution)/shard_map/ppermute | solution.py:27
  59.4 68.4 %collective-permute-start.3 = (bf16[512,1024]{1,0:T(8,128)(2,1)}, bf16[512,1024]{1,0:T(8,128)(2,1)S(1)}, u32[]{:S(2)}, u32[]{:S(2)}) collective-permute-start(bf16[512,1024]{1,0:T(8,128)(2,1)} %collective-permute-done.1), channel_id=1, source_target_pairs={{0,28},{4,0},{8,4},{12,8},{16,12},{20,16},{24,20},{28,24},{1,29},{... | collective-permute-start | bytes 3145736 | tf_op jit(solution)/shard_map/ppermute | solution.py:32
  114.9 60.2 %collective-permute-start.4 = (bf16[512,1024]{1,0:T(8,128)(2,1)S(1)}, bf16[512,1024]{1,0:T(8,128)(2,1)}, u32[]{:S(2)}, u32[]{:S(2)}) collective-permute-start(bf16[512,1024]{1,0:T(8,128)(2,1)S(1)} %collective-permute-done.2), channel_id=1, source_target_pairs={{0,4},{4,8},{8,12},{12,16},{16,20},{20,24},{24,28},{28,0},{1,5},{5... | collective-permute-start | bytes 3145736 | tf_op jit(solution)/shard_map/ppermute | solution.py:27
  117.6 5.4 %copy-start.4 = (s32[16]{0:T(128)S(1)}, s32[16]{0:T(128)}, u32[]{:S(2)}) copy-start(s32[16]{0:T(128)} %param.15) | copy-start | bytes 196
  127.7 294.0 %collective-permute-start.5 = (bf16[512,1024]{1,0:T(8,128)(2,1)S(1)}, bf16[512,1024]{1,0:T(8,128)(2,1)}, u32[]{:S(2)}, u32[]{:S(2)}) collective-permute-start(bf16[512,1024]{1,0:T(8,128)(2,1)S(1)} %collective-permute-done.3), channel_id=1, source_target_pairs={{0,28},{4,0},{8,4},{12,8},{16,12},{20,16},{24,20},{28,24},{1,29},{... | collective-permute-start | bytes 3145736 | tf_op jit(solution)/shard_map/ppermute | solution.py:32
  175.1 248.9 %collective-permute-start.6 = (bf16[512,1024]{1,0:T(8,128)(2,1)}, bf16[512,1024]{1,0:T(8,128)(2,1)}, u32[]{:S(2)}, u32[]{:S(2)}) collective-permute-start(bf16[512,1024]{1,0:T(8,128)(2,1)} %collective-permute-done.4), channel_id=1, source_target_pairs={{0,4},{4,8},{8,12},{12,16},{16,20},{20,24},{24,28},{28,0},{1,5},{5... | collective-permute-start | bytes 3145736 | tf_op jit(solution)/shard_map/ppermute | solution.py:27
  414.6 29.1 %all-to-all-start = ((bf16[8,2,16,2048]{3,2,1,0:T(8,128)(2,1)}), bf16[8,2,16,2048]{3,2,1,0:T(8,128)(2,1)S(1)}, u32[]{:S(2)}, u32[]{:S(2)}) async-start(bf16[8,2,16,2048]{3,2,1,0:T(8,128)(2,1)} %bitcast.2), calls=%async_computation | async-start | bytes 2097152 | tf_op jit(solution)/shard_map/all_to_all | solution.py:73
  472.3 1.4 copy-start
Sparse Core Ops, SparseCore 0:
  8.9 60.9 all-gather.4
  72.1 190.4 all-gather.8
  264.7 123.2 all-gather.6
  389.4 32.6 all-gather.10
